TPU v7x, 128 devices: a whole 4x4x4 slice. The times are simulated.
128 devices in a mesh: grp: 4 (over y_hi, core), blk: 32 (over x, z, y_lo).
Axes of the slice: x: 4, y: 4 (y_hi: 2, y_lo: 2; y = y_hi * 2 + y_lo), z: 4, core: 2. Of those that a mesh axis runs over, the one named last changes fastest.
Arguments:
- tokens: bfloat16 [16384, 2048], P(('grp', 'blk')), may hold values from -6 to 6
- expert_ids: int32 [16384, 6], P(('grp', 'blk')), may hold values from 0 to 7, all different within a row; in each aligned block of 128 rows (0 to 127, 128 to 255, ...) at most 128 rows name the same one
- gate_weights: float32 [16384, 6], P(('grp', 'blk')), may hold values from 0.1 to 1
- w_gate: bfloat16 [8, 1408, 2048], P('grp', 'blk'), may hold values from -0.125 to 0.125
- w_up: bfloat16 [8, 1408, 2048], P('grp', 'blk'), may hold values from -0.125 to 0.125
- w_down: bfloat16 [8, 1408, 2048], P('grp', 'blk'), may hold values from -0.15625 to 0.15625
Outputs:
- mixed: bfloat16 [16384, 2048], P(('grp', 'blk'))
Inputs may be any that keep to these rules, and one draw needn't show every extreme that they name: `expert_ids`: each token names 6 different experts. Among the tokens of one device (aligned blocks of 128 tokens) no expert is named more than 128 times, a bound that some block reaches.
All inputs are finite; a program needn't handle non-finite values.
Results may differ from a plain program's by a relative error of at most 0.008.
Values may be sent and summed in bfloat16 or wider, within the bound.
No kernel may reach another device: no remote copies, remote signals or barrier semaphores. Data moves between devices by JAX's collectives and lax.ppermute only.
A program may use at most 128 MiB of HBM per device.

v0:
```python
import jax
import jax.numpy as jnp
from jax import lax
from jax.sharding import PartitionSpec as P

CAP = 128


def block_hidden(arrived, gate_block, up_block):
    gate_part = jnp.einsum(
        "secd,efd->secf", arrived, gate_block, preferred_element_type=jnp.float32
    )
    up_part = jnp.einsum("secd,efd->secf", arrived, up_block, preferred_element_type=jnp.float32)
    return (jax.nn.silu(gate_part) * up_part).astype(jnp.bfloat16)


def expert_rows(arrived, w_gate, w_up, w_down):
    hidden = block_hidden(
        arrived,
        lax.all_gather(w_gate, "blk", axis=1, tiled=True),
        lax.all_gather(w_up, "blk", axis=1, tiled=True),
    )
    hidden_all = hidden
    hidden = hidden_all
    summed = jnp.einsum(
        "secf,efd->secd",
        hidden,
        lax.all_gather(w_down, "blk", axis=1, tiled=True),
        preferred_element_type=jnp.float32,
    )
    return summed.astype(jnp.bfloat16)


def per_device(tokens, expert_ids, gate_weights, w_gate, w_up, w_down):
    groups = lax.axis_size("grp")
    local_experts = w_gate.shape[0]
    model_width = w_gate.shape[2]
    experts = local_experts * groups
    token_count, top_count = expert_ids.shape
    flat_ids = expert_ids.reshape(-1)
    one_hot = (flat_ids[:, None] == jnp.arange(experts, dtype=jnp.int32)[None, :]).astype(jnp.int32)
    earlier = jnp.cumsum(one_hot, axis=0) - one_hot
    slot_index = jnp.sum(earlier * one_hot, axis=1)
    target = flat_ids * CAP + slot_index
    owner_token = jnp.arange(token_count * top_count, dtype=jnp.int32) // top_count
    slot_owner = jnp.full((experts * CAP,), -1, jnp.int32).at[target].set(owner_token)
    slot_filled = slot_owner >= 0
    token_rows = jnp.where(
        slot_filled[:, None], tokens[jnp.maximum(slot_owner, 0)], jnp.zeros((), jnp.bfloat16)
    )
    outgoing = token_rows.reshape(groups, local_experts, CAP, model_width)
    arrived_out = expert_rows(
        lax.all_to_all(outgoing, "grp", split_axis=0, concat_axis=0, tiled=True),
        w_gate,
        w_up,
        w_down,
    )
    returned = lax.all_to_all(arrived_out, "grp", split_axis=0, concat_axis=0, tiled=True)
    returned_flat = returned.reshape(experts * CAP, model_width)
    picked = returned_flat[target].reshape(token_count, top_count, model_width)
    mixed = jnp.einsum("tk,tkd->td", gate_weights, picked.astype(jnp.float32))
    return mixed.astype(jnp.bfloat16)


def solution(mesh):
    return jax.shard_map(
        per_device,
        mesh=mesh,
        in_specs=(
            P(("grp", "blk"), None),
            P(("grp", "blk"), None),
            P(("grp", "blk"), None),
            P("grp", "blk", None),
            P("grp", "blk", None),
            P("grp", "blk", None),
        ),
        out_specs=P(("grp", "blk"), None),
        check_vma=False,
    )
```

profile of v0, /device:TPU:0, one launch (start us, length us, event | category | flops | bytes accessed | tf_op | source)
XLA Modules:
  0.0 915.4 jit_solution(15056221233799316622)
XLA Ops:
  6.5 0.7 all-gather.4.cloned.1.call-update
  7.3 0.7 all-gather.6.cloned.1.call-update
  8.1 0.7 all-gather.8.cloned.1.call-update
  8.7 0.8 copy.22
  9.8 1.7 reduce-window.6
  11.8 0.2 reduce-window.9
  12.0 0.7 broadcast_multiply_fusion
  13.1 3.4 scatter_custom_fusion
  16.5 6.0 gather_fusion
  22.5 2.5 broadcast_select_fusion
  25.1 118.8 %all_to_all.10 = bf16[4,2,128,2048]{3,2,1,0:T(8,128)(2,1)} all-to-all(bf16[4,2,128,2048]{3,2,1,0:T(8,128)(2,1)S(1)} %broadcast_select_fusion), channel_id=1, replica_groups=mesh['grp'=4,'blk'=32] {'grp'}, dimensions={0} | all-to-all | bytes 8388608 | tf_op jit(solution)/shard_map/all_to_all | solution.py:53
  143.9 164.7 %all-gather.4.cloned.1.call-done = bf16[2,1408,2048]{2,0,1:T(2,128)(2,1)} async-done(((bf16[2,44,2048]{2,0,1:T(2,128)(2,1)}), bf16[2,1408,2048]{2,0,1:T(2,128)(2,1)}) %all-gather.4.cloned.1.call-update) | async-done | bytes 11534352 | tf_op jit(solution)/shard_map/all_gather | solution.py:20
  308.6 22.0 %fusion.4 = f32[2,4,128,1408]{3,2,1,0:T(8,128)} fusion(bf16[2,1408,2048,1]{2,0,1,3:T(2,128)(2,1)} %bitcast.45, bf16[4,2,128,2048]{3,2,1,0:T(8,128)(2,1)} %all_to_all.10), kind=kOutput, calls=%fused_computation.7 | convolution fusion | flops 5905580032 | bytes 21495808 | tf_op jit(solution)/shard_map/secd,efd->secf/dot_general | solution.py:10
  330.6 232.8 %all-gather.6.cloned.1.call-done = bf16[2,1408,2048]{2,0,1:T(2,128)(2,1)} async-done(((bf16[2,44,2048]{2,0,1:T(2,128)(2,1)}), bf16[2,1408,2048]{2,0,1:T(2,128)(2,1)}) %all-gather.6.cloned.1.call-update) | async-done | bytes 11534352 | tf_op jit(solution)/shard_map/all_gather | solution.py:21
  563.4 19.3 %fusion.6 = bf16[4,2,128,1408]{3,2,0,1:T(8,128)(2,1)S(1)} fusion(f32[2,4,128,1408]{3,2,1,0:T(8,128)} %fusion.4, bf16[2,1408,2048,1]{2,0,1,3:T(2,128)(2,1)} %bitcast.46, bf16[4,2,128,2048]{3,2,1,0:T(8,128)(2,1)} %all_to_all.10), kind=kOutput, calls=%fused_computation.10 | convolution fusion | flops 5914230784 | bytes 24379392 | tf_op jit(solution)/shard_map/secd,efd->secf/dot_general | solution.py:13
  582.8 235.5 %all-gather.8.cloned.1.call-done = bf16[2,1408,2048]{2,0,1:T(2,128)(2,1)} async-done(((bf16[2,44,2048]{2,0,1:T(2,128)(2,1)}), bf16[2,1408,2048]{2,0,1:T(2,128)(2,1)}) %all-gather.8.cloned.1.call-update) | async-done | bytes 11534352 | tf_op jit(solution)/shard_map/all_gather | solution.py:28
  818.3 12.5 %convert_bitcast_fusion = bf16[4,2,128,2048]{3,2,0,1:T(8,128)(2,1)S(1)} fusion(bf16[4,2,128,1408]{3,2,0,1:T(8,128)(2,1)S(1)} %fusion.6, bf16[2,1408,2048,1]{2,0,1,3:T(2,128)(2,1)} %bitcast.47), kind=kOutput, calls=%fused_computation.16 | convolution fusion | flops 5907677184 | bytes 18612224 | tf_op jit(solution)/shard_map/secf,efd->secd/dot_general | solution.py:25
  830.8 2.5 copy.31
  833.3 5.2 all-to-all-start.1
  838.7 49.5 %all-to-all-done.1 = bf16[4,2,128,2048]{3,2,1,0:T(8,128)(2,1)} async-done(((bf16[4,2,128,2048]{3,2,1,0:T(8,128)(2,1)}), bf16[4,2,128,2048]{3,2,1,0:T(8,128)(2,1)}, u32[]{:S(2)}, u32[]{:S(2)}) %all-to-all-start.1) | async-done | bytes 4194336 | tf_op jit(solution)/shard_map/all_to_all | solution.py:58
  888.2 9.8 %gather_fusion.1 = bf16[768,2048]{1,0:T(8,128)(2,1)} fusion(bf16[1024,2048]{1,0:T(8,128)(2,1)} %bitcast.10, s32[1024]{0:T(1024)S(1)} %pad_clamp_fusion), kind=kCustom, calls=%fused_computation.1 | custom fusion | bytes 6294528 | tf_op jit(solution)/shard_map/gather | solution.py:60
  898.1 6.3 reshape.62
  904.4 3.4 fusion.25
  907.8 1.1 copy.58
  (25 shorter events, 1.2 us)
Async XLA Ops:
  6.5 10.0 %copy-start = (bf16[128,2048]{1,0:T(8,128)(2,1)S(1)}, bf16[128,2048]{1,0:T(8,128)(2,1)}, u32[]{:S(2)}) copy-start(bf16[128,2048]{1,0:T(8,128)(2,1)} %param.6) | copy-start | bytes 1572868
  6.5 302.1 %all-gather.4.cloned.1.call-start = ((), (), s32[]{:S(2)}) async-start(), calls=%async_computation.2 | async-start | bytes 11894784 | tf_op jit(solution)/shard_map/all_gather | solution.py:20
  7.3 556.2 %all-gather.6.cloned.1.call-start = ((), (), s32[]{:S(2)}) async-start(), calls=%async_computation.3 | async-start | bytes 11894784 | tf_op jit(solution)/shard_map/all_gather | solution.py:21
  8.0 810.3 %all-gather.8.cloned.1.call-start = ((), (), s32[]{:S(2)}) async-start(), calls=%async_computation.4 | async-start | bytes 11894784 | tf_op jit(solution)/shard_map/all_gather | solution.py:28
  833.3 5.2 copy-start.2
  833.3 54.9 %all-to-all-start.1 = ((bf16[4,2,128,2048]{3,2,1,0:T(8,128)(2,1)}), bf16[4,2,128,2048]{3,2,1,0:T(8,128)(2,1)}, u32[]{:S(2)}, u32[]{:S(2)}) async-start(bf16[4,2,128,2048]{3,2,1,0:T(8,128)(2,1)} %copy.31), calls=%async_computation.1 | async-start | bytes 8388608 | tf_op jit(solution)/shard_map/all_to_all | solution.py:58
  898.1 10.8 %copy-start.1 = (bf16[128,2048]{1,0:T(8,128)(2,1)S(1)}, bf16[128,2048]{1,0:T(8,128)(2,1)}, u32[]{:S(2)}) copy-start(bf16[128,2048]{1,0:T(8,128)(2,1)} %param.6) | copy-start | bytes 1572868
Sparse Core Ops, SparseCore 0:
  9.0 299.5 all-gather.3
  310.2 253.1 all-gather.5
  565.1 253.1 all-gather.7
where the time goes:
time: 917 us; the launch traced here: 915 us
  waiting for transfers between devices  685 us (75%)
  blocking collectives  119 us (13%)
  matrix products  57.3 us (6%)
  local copies, waits for them, and re-layouts  30.9 us (3%)
  between operations  13.2 us (1%)
    all_gather x1, waiting for transfers between devices, expert_rows(): lax.all_gather(w_down, 'blk', axis=1, tiled=True)  236 us
    all_gather x1, waiting for transfers between devices, expert_rows(): lax.all_gather(w_up, 'blk', axis=1, tiled=True)  233 us
    all_gather x1, waiting for transfers between devices, expert_rows(): lax.all_gather(w_gate, 'blk', axis=1, tiled=True)  165 us
    all_to_all x1, blocking collectives, per_device(): lax.all_to_all(outgoing, 'grp', split_axis=0, concat_axis=0, tiled=True)  119 us
    all_to_all x1, waiting for transfers between devices, per_device(): lax.all_to_all(arrived_out, 'grp', split_axis=0, concat_axis=0, tiled=True)  49.5 us
    dot_general x1, matrix products, block_hidden(): jnp.einsum('secd,efd->secf', arrived, gate_block, preferred_element_type=...  22 us
    dot_general x1, matrix products, block_hidden(): jnp.einsum('secd,efd->secf', arrived, up_block, preferred_element_type=jn...  19.3 us
  transfers between devices with their start and end apart: 4, of which 4 were waited for; matrix products, arithmetic and copies ran while one was open for 6% of the time, Pallas kernels for 0%

commit v1 on v0

v1 whole, which is shorter than its diff:
```python
import jax
import jax.numpy as jnp
from jax import lax
from jax.sharding import Mesh
from jax.sharding import PartitionSpec as P

POOL = ("grp", "ylo")
PLANE = ("x", "z")


def expert_weights(w, ylo):
    keep = lax.dynamic_index_in_dim(w, ylo, axis=0, keepdims=False)
    send = lax.dynamic_index_in_dim(w, 1 - ylo, axis=0, keepdims=False)
    got = lax.ppermute(send, "ylo", perm=[(0, 1), (1, 0)])
    pair = jnp.stack([keep, got])
    full = lax.all_gather(pair, PLANE, axis=0, tiled=False)
    return full.reshape(-1, w.shape[-1])


def per_device(tokens, expert_ids, gate_weights, w_gate, w_up, w_down):
    ylo = lax.axis_index("ylo")
    pool = lax.axis_size("grp") * lax.axis_size("ylo")
    me = lax.axis_index("grp") * lax.axis_size("ylo") + ylo
    token_count, model_width = tokens.shape

    gate_full = expert_weights(w_gate, ylo)
    up_full = expert_weights(w_up, ylo)
    down_full = expert_weights(w_down, ylo)

    rows = lax.all_gather(tokens, POOL, axis=0, tiled=True)
    gate_part = jnp.dot(rows, gate_full.T, preferred_element_type=jnp.float32)
    up_part = jnp.dot(rows, up_full.T, preferred_element_type=jnp.float32)
    hidden = (jax.nn.silu(gate_part) * up_part).astype(jnp.bfloat16)
    out = jnp.dot(hidden, down_full, preferred_element_type=jnp.float32).astype(jnp.bfloat16)

    back = lax.all_to_all(
        out.reshape(pool, token_count, model_width), POOL, split_axis=0, concat_axis=0, tiled=True
    )
    experts = jnp.arange(pool, dtype=jnp.int32)
    weight = jnp.sum(
        jnp.where(expert_ids[:, :, None] == experts[None, None, :], gate_weights[:, :, None], 0.0),
        axis=1,
    )
    del me
    mixed = jnp.einsum("te,etd->td", weight, back.astype(jnp.float32))
    return mixed.astype(jnp.bfloat16)


def solution(mesh):
    grp, blk = mesh.devices.shape
    ylo = 2
    fine = Mesh(
        mesh.devices.reshape(grp, 4, blk // (4 * ylo), ylo), ("grp", "x", "z", "ylo")
    )
    rows = P(("grp", "x", "z", "ylo"), None)
    weights = P("grp", ("x", "z", "ylo"), None)
    return jax.shard_map(
        per_device,
        mesh=fine,
        in_specs=(rows, rows, rows, weights, weights, weights),
        out_specs=rows,
        check_vma=False,
    )
```

time: 917 us -> 380 us (0.41)
  waiting for transfers between devices: 685 us -> 285 us
  blocking collectives: 119 us -> 0 us
  matrix products: 57.3 us -> 37.8 us
    all_gather x3 -> x4, waiting for transfers between devices: 633 us -> 223 us  [the longest x3 160 us: expert_weights(): full = lax.all_gather(pair, PLANE, axis=0, tiled=False)]
    all_to_all x1 -> x0, blocking collectives: 119 us -> none  [per_device(): lax.all_to_all(outgoing, 'grp', split_axis=0, concat_axis=0, tiled=True)]
    dot_general x4 -> x3, matrix products: 57.3 us -> 37.8 us  [the longest x1 21.1 us: per_device(): jnp.dot(hidden, down_full, preferred_element_type=jnp.float32)]
    reshape x1 -> x3, local copies, waits for them, and re-layouts: 6.31 us -> 23.9 us  [expert_weights(): return full.reshape(-1, w.shape[-1])]
    gather x2 -> x0, local copies, waits for them, and re-layouts: 15.9 us -> none  [the longest x1 9.85 us: per_device(): picked = returned_flat[target].reshape(token_count, top_count, model_width)]
    ppermute x0 -> x3, waiting for transfers between devices: none -> 12.5 us  [expert_weights(): got = lax.ppermute(send, 'ylo', perm=[(0, 1), (1, 0)])]
  transfers between devices with their start and end apart: 4 -> 8, of which waited for: 4 -> 8; matrix products, arithmetic and copies ran while one was open for 6% -> 7% of each run, Pallas kernels for 0% -> 0%
where the time goes in v1:
time: 380 us; the launch traced here: 378 us
  waiting for transfers between devices  285 us (75%)
  matrix products  37.8 us (10%)
  local copies, waits for them, and re-layouts  29.3 us (8%)
  between operations  13.2 us (3%)
  starting transfers between devices  10.6 us (3%)
    all_gather x3, waiting for transfers between devices, expert_weights(): full = lax.all_gather(pair, PLANE, axis=0, tiled=False)  160 us
    all_gather x1, waiting for transfers between devices, per_device(): rows = lax.all_gather(tokens, POOL, axis=0, tiled=True)  63.2 us
    all_to_all x1, waiting for transfers between devices, per_device(): lax.all_to_all(out.reshape(pool, token_count, model_width), POOL, split_a...  49.3 us
    reshape x3, local copies, waits for them, and re-layouts, expert_weights(): return full.reshape(-1, w.shape[-1])  23.9 us
    dot_general x1, matrix products, per_device(): jnp.dot(hidden, down_full, preferred_element_type=jnp.float32)  21.1 us
    ppermute x3, waiting for transfers between devices, expert_weights(): got = lax.ppermute(send, 'ylo', perm=[(0, 1), (1, 0)])  12.5 us
    dot_general x1, matrix products, per_device(): up_part = jnp.dot(rows, up_full.T, preferred_element_type=jnp.float32)  11.4 us
  transfers between devices with their start and end apart: 8, of which 8 were waited for; matrix products, arithmetic and copies ran while one was open for 7% of the time, Pallas kernels for 0%

profile of v1, /device:TPU:0, one launch (start us, length us, event | category | flops | bytes accessed | tf_op | source)
XLA Modules:
  0.0 378.4 jit_solution(16751027924030423068)
XLA Ops:
  6.5 2.8 constant_dynamic-slice_fusion.1
  9.5 1.7 collective-permute-start.1
  11.4 4.8 %collective-permute-done.1 = bf16[44,2048]{1,0:T(8,128)(2,1)S(1)} collective-permute-done((bf16[44,2048]{1,0:T(8,128)(2,1)S(1)}, bf16[44,2048]{1,0:T(8,128)(2,1)S(1)}, u32[]{:S(2)}, u32[]{:S(2)}) %collective-permute-start.1) | collective-permute-done | bytes 180256 | tf_op jit(solution)/shard_map/ppermute | solution.py:14
  16.1 0.8 pad_maximum_fusion.1
  17.1 1.8 collective-permute-start.2
  19.1 3.9 %collective-permute-done.2 = bf16[44,2048]{1,0:T(8,128)(2,1)S(1)} collective-permute-done((bf16[44,2048]{1,0:T(8,128)(2,1)S(1)}, bf16[44,2048]{1,0:T(8,128)(2,1)S(1)}, u32[]{:S(2)}, u32[]{:S(2)}) %collective-permute-start.2) | collective-permute-done | bytes 180256 | tf_op jit(solution)/shard_map/ppermute | solution.py:14
  23.0 0.8 pad_maximum_fusion.2
  23.8 0.8 constant_dynamic-slice_fusion.5
  24.7 1.8 collective-permute-start
  26.7 3.8 %collective-permute-done = bf16[44,2048]{1,0:T(8,128)(2,1)S(1)} collective-permute-done((bf16[44,2048]{1,0:T(8,128)(2,1)S(1)}, bf16[44,2048]{1,0:T(8,128)(2,1)S(1)}, u32[]{:S(2)}, u32[]{:S(2)}) %collective-permute-start) | collective-permute-done | bytes 180256 | tf_op jit(solution)/shard_map/ppermute | solution.py:14
  30.5 0.8 pad_maximum_fusion
  31.9 49.2 %all-gather.12.cloned.1.call-done = bf16[32,44,2048]{2,1,0:T(8,128)(2,1)} async-done(((bf16[2,44,2048]{2,1,0:T(8,128)(2,1)}), bf16[32,44,2048]{2,1,0:T(8,128)(2,1)}) %all-gather.12.cloned.1.call-update) | async-done | bytes 5767184 | tf_op jit(solution)/shard_map/all_gather | solution.py:16
  81.1 8.0 %reshape.15 = bf16[1408,2048]{1,0:T(8,128)(2,1)} reshape(bf16[32,44,2048]{2,1,0:T(8,128)(2,1)} %all-gather.12.cloned.1.call-done) | data formatting | bytes 11534336 | tf_op jit(solution)/shard_map/reshape | solution.py:17
  89.1 55.2 %all-gather.14.cloned.1.call-done = bf16[32,44,2048]{2,1,0:T(8,128)(2,1)} async-done(((bf16[2,44,2048]{2,1,0:T(8,128)(2,1)}), bf16[32,44,2048]{2,1,0:T(8,128)(2,1)}) %all-gather.14.cloned.1.call-update) | async-done | bytes 5767184 | tf_op jit(solution)/shard_map/all_gather | solution.py:16
  144.3 7.9 %reshape.16 = bf16[1408,2048]{1,0:T(8,128)(2,1)} reshape(bf16[32,44,2048]{2,1,0:T(8,128)(2,1)} %all-gather.14.cloned.1.call-done) | data formatting | bytes 11534336 | tf_op jit(solution)/shard_map/reshape | solution.py:17
  152.2 55.3 %all-gather.10.cloned.1.call-done = bf16[32,44,2048]{2,1,0:T(8,128)(2,1)} async-done(((bf16[2,44,2048]{2,1,0:T(8,128)(2,1)}), bf16[32,44,2048]{2,1,0:T(8,128)(2,1)}) %all-gather.10.cloned.1.call-update) | async-done | bytes 5767184 | tf_op jit(solution)/shard_map/all_gather | solution.py:16
  207.5 7.9 %reshape.14 = bf16[1408,2048]{1,0:T(8,128)(2,1)} reshape(bf16[32,44,2048]{2,1,0:T(8,128)(2,1)} %all-gather.10.cloned.1.call-done) | data formatting | bytes 11534336 | tf_op jit(solution)/shard_map/reshape | solution.py:17
  215.4 63.2 %all-gather.8.cloned.1.call-done = bf16[1024,2048]{1,0:T(8,128)(2,1)} async-done(((bf16[128,2048]{1,0:T(8,128)(2,1)}), bf16[1024,2048]{1,0:T(8,128)(2,1)}) %all-gather.8.cloned.1.call-update) | async-done | bytes 4194320 | tf_op jit(solution)/shard_map/all_gather | solution.py:30
  278.6 11.4 %fusion.6 = f32[1408,1024]{1,0:T(8,128)} fusion(bf16[1408,2048]{1,0:T(8,128)(2,1)} %reshape.15, bf16[1024,2048]{1,0:T(8,128)(2,1)} %all-gather.8.cloned.1.call-done), kind=kOutput, calls=%fused_computation.25 | convolution fusion | flops 5905580032 | bytes 15728640 | tf_op jit(solution)/shard_map/dot_general | solution.py:32
  290.0 21.1 %convolution_convert_fusion = bf16[1024,2048]{1,0:T(8,128)(2,1)} fusion(bf16[1408,2048]{1,0:T(8,128)(2,1)} %reshape.16, f32[1408,1024]{1,0:T(8,128)} %fusion.6, bf16[1408,2048]{1,0:T(8,128)(2,1)} %reshape.14, bf16[1024,2048]{1,0:T(8,128)(2,1)} %all-gather.8.cloned.1.call-done), kind=kOutput, calls=%fused_computation.9 | convolution fusion | flops 11821907968 | bytes 25690112 | tf_op jit(solution)/shard_map/dot_general | solution.py:34
  311.1 4.9 %all-to-all-start = ((bf16[8,128,2048]{2,1,0:T(8,128)(2,1)}), bf16[8,128,2048]{2,1,0:T(8,128)(2,1)}, u32[]{:S(2)}, u32[]{:S(2)}) async-start(bf16[8,128,2048]{2,1,0:T(8,128)(2,1)} %bitcast.57), calls=%async_computation | async-start | bytes 8388608 | tf_op jit(solution)/shard_map/all_to_all | solution.py:36
  316.1 49.3 %all-to-all-done = bf16[8,128,2048]{2,1,0:T(8,128)(2,1)} async-done(((bf16[8,128,2048]{2,1,0:T(8,128)(2,1)}), bf16[8,128,2048]{2,1,0:T(8,128)(2,1)}, u32[]{:S(2)}, u32[]{:S(2)}) %all-to-all-start) | async-done | bytes 4194336 | tf_op jit(solution)/shard_map/all_to_all | solution.py:36
  365.5 5.3 %fusion.4 = bf16[128,1,2048]{2,1,0:T(2,128)(2,1)S(1)} fusion(bf16[128,8,1]{1,2,0:T(2,128)(2,1)S(1)} %copy.31, bf16[8,128,2048]{2,1,0:T(8,128)(2,1)} %all-to-all-done), kind=kOutput, calls=%fused_computation.7 | convolution fusion | flops 4194304 | bytes 4720640 | tf_op jit(solution)/shard_map/te,etd->td/dot_general | solution.py:45
  370.8 1.1 copy.46
  (22 shorter events, 1.5 us)
Async XLA Ops:
  6.5 17.3 %copy-start = (bf16[2,44,2048]{2,0,1:T(2,128)(2,1)S(1)}, bf16[2,44,2048]{2,0,1:T(2,128)(2,1)}, u32[]{:S(2)}) copy-start(bf16[2,44,2048]{2,0,1:T(2,128)(2,1)} %param.9) | copy-start | bytes 1081348
  6.5 74.5 %all-gather.12.cloned.1.call-start = ((), (), s32[]{:S(2)}) async-start(), calls=%async_computation.3 | async-start | bytes 6684672 | tf_op jit(solution)/shard_map/all_gather | solution.py:16
  9.5 6.6 %collective-permute-start.1 = (bf16[44,2048]{1,0:T(8,128)(2,1)S(1)}, bf16[44,2048]{1,0:T(8,128)(2,1)S(1)}, u32[]{:S(2)}, u32[]{:S(2)}) collective-permute-start(bf16[44,2048]{1,0:T(8,128)(2,1)S(1)} %bitcast.60), channel_id=1, source_target_pairs={{0,1},{1,0},{2,3},{3,2},{4,5},{5,4},{6,7},{7,6},{8,9},{9,8},{10,11... | collective-permute-start | bytes 540680 | tf_op jit(solution)/shard_map/ppermute | solution.py:14
  17.0 127.3 %all-gather.14.cloned.1.call-start = ((), (), s32[]{:S(2)}) async-start(), calls=%async_computation.4 | async-start | bytes 6684672 | tf_op jit(solution)/shard_map/all_gather | solution.py:16
  17.1 5.8 %collective-permute-start.2 = (bf16[44,2048]{1,0:T(8,128)(2,1)S(1)}, bf16[44,2048]{1,0:T(8,128)(2,1)S(1)}, u32[]{:S(2)}, u32[]{:S(2)}) collective-permute-start(bf16[44,2048]{1,0:T(8,128)(2,1)S(1)} %bitcast.58), channel_id=1, source_target_pairs={{0,1},{1,0},{2,3},{3,2},{4,5},{5,4},{6,7},{7,6},{8,9},{9,8},{10,11... | collective-permute-start | bytes 540680 | tf_op jit(solution)/shard_map/ppermute | solution.py:14
  23.8 183.7 %all-gather.10.cloned.1.call-start = ((), (), s32[]{:S(2)}) async-start(), calls=%async_computation.2 | async-start | bytes 6684672 | tf_op jit(solution)/shard_map/all_gather | solution.py:16
  24.7 5.7 %collective-permute-start = (bf16[44,2048]{1,0:T(8,128)(2,1)S(1)}, bf16[44,2048]{1,0:T(8,128)(2,1)S(1)}, u32[]{:S(2)}, u32[]{:S(2)}) collective-permute-start(bf16[44,2048]{1,0:T(8,128)(2,1)S(1)} %bitcast.59), channel_id=1, source_target_pairs={{0,1},{1,0},{2,3},{3,2},{4,5},{5,4},{6,7},{7,6},{8,9},{9,8},{10,11... | collective-permute-start | bytes 540680 | tf_op jit(solution)/shard_map/ppermute | solution.py:14
  31.3 247.3 %all-gather.8.cloned.1.call-start = ((), (), s32[]{:S(2)}) async-start(), calls=%async_computation.1 | async-start | bytes 4718592 | tf_op jit(solution)/shard_map/all_gather | solution.py:30
  311.0 4.9 %copy-start.1 = (f32[128,6]{0,1:T(8,128)S(1)}, f32[128,6]{0,1:T(8,128)}, u32[]{:S(2)}) copy-start(f32[128,6]{0,1:T(8,128)} %param.8) | copy-start | bytes 9220
  311.1 4.9 %copy-start.2 = (s32[128,6]{0,1:T(8,128)S(1)}, s32[128,6]{0,1:T(8,128)}, u32[]{:S(2)}) copy-start(s32[128,6]{0,1:T(8,128)} %param.7) | copy-start | bytes 9220
  311.1 54.4 %all-to-all-start = ((bf16[8,128,2048]{2,1,0:T(8,128)(2,1)}), bf16[8,128,2048]{2,1,0:T(8,128)(2,1)}, u32[]{:S(2)}, u32[]{:S(2)}) async-start(bf16[8,128,2048]{2,1,0:T(8,128)(2,1)} %bitcast.57), calls=%async_computation | async-start | bytes 8388608 | tf_op jit(solution)/shard_map/all_to_all | solution.py:36
Sparse Core Ops, SparseCore 0:
  17.1 63.9 all-gather.11
  83.2 60.9 all-gather.13
  146.5 60.9 all-gather.9
  209.0 69.5 all-gather.7

commit v2 on v1

v2 whole, which is shorter than its diff:
```python
import jax
import jax.numpy as jnp
from jax import lax
from jax.sharding import Mesh
from jax.sharding import PartitionSpec as P

CHIPS = ("yhi", "ylo")
PLANE = ("x", "z")
SWAP = [(0, 1), (1, 0)]


def expert_weights(w, ylo):
    keep = lax.dynamic_index_in_dim(w, ylo, axis=0, keepdims=False)
    send = lax.dynamic_index_in_dim(w, 1 - ylo, axis=0, keepdims=False)
    got = lax.ppermute(send, "ylo", perm=SWAP)
    pair = jnp.stack([keep, got])
    full = lax.all_gather(pair, PLANE, axis=0, tiled=False)
    return full.reshape(-1, w.shape[-1])


def spread(value, chips):
    sent = jnp.broadcast_to(value[None], (chips,) + value.shape)
    mine = lax.all_to_all(sent, CHIPS, split_axis=0, concat_axis=0, tiled=True)
    other = lax.ppermute(mine, "core", perm=SWAP)
    return mine, other


def per_device(tokens, expert_ids, gate_weights, w_gate, w_up, w_down):
    ylo = lax.axis_index("ylo")
    chips = lax.axis_size("yhi") * lax.axis_size("ylo")
    expert = (lax.axis_index("yhi") * lax.axis_size("core") + lax.axis_index("core")) * 2 + ylo
    token_count, model_width = tokens.shape

    gate_full = expert_weights(w_gate, ylo)
    up_full = expert_weights(w_up, ylo)
    down_full = expert_weights(w_down, ylo)

    experts = jnp.arange(lax.axis_size("core") * chips, dtype=jnp.int32)
    weight = jnp.sum(
        jnp.where(expert_ids[:, :, None] == experts, gate_weights[:, :, None], 0.0), axis=1
    )
    rows_mine, rows_other = spread(tokens, chips)
    weight_mine, weight_other = spread(weight, chips)
    rows = jnp.concatenate([rows_mine, rows_other]).reshape(-1, model_width)
    table = jnp.concatenate([weight_mine, weight_other]).reshape(-1, experts.shape[0])
    scale = lax.dynamic_index_in_dim(table, expert, axis=1, keepdims=True)

    gate_part = jnp.dot(rows, gate_full.T, preferred_element_type=jnp.float32)
    up_part = jnp.dot(rows, up_full.T, preferred_element_type=jnp.float32)
    hidden = (jax.nn.silu(gate_part) * up_part).astype(jnp.bfloat16)
    out = jnp.dot(hidden, down_full, preferred_element_type=jnp.float32).astype(jnp.bfloat16)
    scaled = (out.astype(jnp.float32) * scale).reshape(2, chips, token_count, model_width)

    partner = lax.ppermute(scaled[1], "core", perm=SWAP)
    partial = (scaled[0] + partner).astype(jnp.bfloat16)
    back = lax.all_to_all(partial, CHIPS, split_axis=0, concat_axis=0, tiled=True)
    mixed = jnp.sum(back.astype(jnp.float32), axis=0)
    return mixed.astype(jnp.bfloat16)


def solution(mesh):
    grp, blk = mesh.devices.shape
    ylo = 2
    fine = Mesh(
        mesh.devices.reshape(2, grp // 2, 4, blk // (4 * ylo), ylo),
        ("yhi", "core", "x", "z", "ylo"),
    )
    rows = P(("yhi", "core", "x", "z", "ylo"), None)
    weights = P(("yhi", "core"), ("x", "z", "ylo"), None)
    return jax.shard_map(
        per_device,
        mesh=fine,
        in_specs=(rows, rows, rows, weights, weights, weights),
        out_specs=rows,
        check_vma=False,
    )
```

time: 380 us -> 288 us (0.76)
  waiting for transfers between devices: 285 us -> 126 us
  blocking collectives: 0 us -> 66.2 us
  other arithmetic: 2.38 us -> 8.71 us
  starting transfers between devices: 10.6 us -> 5.55 us
  matrix products: 37.8 us -> 33.3 us
  local copies, waits for them, and re-layouts: 29.3 us -> 33.7 us
    all_to_all x0 -> x3, blocking collectives: none -> 66.2 us  [the longest x2 35.5 us: spread(): mine = lax.all_to_all(sent, CHIPS, split_axis=0, concat_axis=0, tiled=True)]
    all_gather x1 -> x0, waiting for transfers between devices: 63.2 us -> none  [per_device(): rows = lax.all_gather(tokens, POOL, axis=0, tiled=True)]
    all_gather x3, waiting for transfers between devices: 160 us -> 105 us  [expert_weights(): full = lax.all_gather(pair, PLANE, axis=0, tiled=False)]
    all_to_all x1 -> x0, waiting for transfers between devices: 49.3 us -> none  [per_device(): lax.all_to_all(out.reshape(pool, token_count, model_width), POOL, split_a...]
    ppermute x3 -> x6, waiting for transfers between devices: 12.5 us -> 20.9 us  [the longest x3 12.5 us: expert_weights(): got = lax.ppermute(send, 'ylo', perm=SWAP)]
    all_to_all x1 -> x0, starting transfers between devices: 4.91 us -> none  [per_device(): lax.all_to_all(out.reshape(pool, token_count, model_width), POOL, split_a...]
    dot_general x2 -> x1, matrix products: 16.7 us -> 11.8 us  [per_device(): gate_part = jnp.dot(rows, gate_full.T, preferred_element_type=jnp.float32)]
    slice x0 -> x1, local copies, waits for them, and re-layouts: none -> 4.05 us  [per_device(): partner = lax.ppermute(scaled[1], 'core', perm=SWAP)]
  transfers between devices with their start and end apart: 8 -> 9, of which waited for: 8 -> 8; matrix products, arithmetic and copies ran while one was open for 7% -> 13% of each run, Pallas kernels for 0% -> 0%
where the time goes in v2:
time: 288 us; the launch traced here: 287 us
  waiting for transfers between devices  126 us (44%)
  blocking collectives  66.2 us (23%)
  local copies, waits for them, and re-layouts  33.7 us (12%)
  matrix products  33.3 us (12%)
  between operations  13.2 us (5%)
  other arithmetic  8.71 us (3%)
  starting transfers between devices  5.55 us (2%)
    all_gather x3, waiting for transfers between devices, expert_weights(): full = lax.all_gather(pair, PLANE, axis=0, tiled=False)  105 us
    all_to_all x2, blocking collectives, spread(): mine = lax.all_to_all(sent, CHIPS, split_axis=0, concat_axis=0, tiled=True)  35.5 us
    all_to_all x1, blocking collectives, per_device(): lax.all_to_all(partial, CHIPS, split_axis=0, concat_axis=0, tiled=True)  30.7 us
    reshape x3, local copies, waits for them, and re-layouts, expert_weights(): return full.reshape(-1, w.shape[-1])  24 us
    dot_general x1, matrix products, per_device(): jnp.dot(hidden, down_full, preferred_element_type=jnp.float32)  21.4 us
    ppermute x3, waiting for transfers between devices, expert_weights(): got = lax.ppermute(send, 'ylo', perm=SWAP)  12.5 us
    dot_general x1, matrix products, per_device(): gate_part = jnp.dot(rows, gate_full.T, preferred_element_type=jnp.float32)  11.8 us
    ppermute x1, waiting for transfers between devices, per_device(): partner = lax.ppermute(scaled[1], 'core', perm=SWAP)  7.15 us
  transfers between devices with their start and end apart: 9, of which 8 were waited for; matrix products, arithmetic and copies ran while one was open for 13% of the time, Pallas kernels for 0%

profile of v2, /device:TPU:0, one launch (start us, length us, event | category | flops | bytes accessed | tf_op | source)
XLA Modules:
  0.0 286.9 jit_solution(11992764743097563078)
XLA Ops:
  6.5 1.9 constant_dynamic-slice_fusion.6
  8.6 1.7 collective-permute-start.1
  10.4 4.8 %collective-permute-done.1 = bf16[44,2048]{1,0:T(8,128)(2,1)S(1)} collective-permute-done((bf16[44,2048]{1,0:T(8,128)(2,1)S(1)}, bf16[44,2048]{1,0:T(8,128)(2,1)S(1)}, u32[]{:S(2)}, u32[]{:S(2)}) %collective-permute-start.1) | collective-permute-done | bytes 180256 | tf_op jit(solution)/shard_map/ppermute | solution.py:15
  16.1 2.8 constant_dynamic-slice_fusion.2
  19.1 1.8 collective-permute-start.2
  21.0 3.9 %collective-permute-done.2 = bf16[44,2048]{1,0:T(8,128)(2,1)S(1)} collective-permute-done((bf16[44,2048]{1,0:T(8,128)(2,1)S(1)}, bf16[44,2048]{1,0:T(8,128)(2,1)S(1)}, u32[]{:S(2)}, u32[]{:S(2)}) %collective-permute-start.2) | collective-permute-done | bytes 180256 | tf_op jit(solution)/shard_map/ppermute | solution.py:15
  25.9 1.8 collective-permute-start.3
  27.8 3.8 %collective-permute-done.3 = bf16[44,2048]{1,0:T(8,128)(2,1)S(1)} collective-permute-done((bf16[44,2048]{1,0:T(8,128)(2,1)S(1)}, bf16[44,2048]{1,0:T(8,128)(2,1)S(1)}, u32[]{:S(2)}, u32[]{:S(2)}) %collective-permute-start.3) | collective-permute-done | bytes 180256 | tf_op jit(solution)/shard_map/ppermute | solution.py:15
  32.7 27.8 %all_to_all.15 = bf16[4,128,2048]{2,1,0:T(8,128)(2,1)S(1)} all-to-all(bf16[4,128,2048]{2,1,0:T(8,128)(2,1)S(1)} %broadcast_in_dim.16), channel_id=1, replica_groups=mesh['yhi'=2,'core'=2,'x'=4,'z'=4,'ylo'=2] {'yhi','ylo'}, dimensions={0} | all-to-all | bytes 4194304 | tf_op jit(solution)/shard_map/all_to_all | solution.py:23
  60.6 7.7 %all_to_all.16 = f32[4,128,8]{1,2,0:T(8,128)S(1)} all-to-all(f32[4,128,8]{1,2,0:T(8,128)S(1)} %broadcast_in_dim.30), channel_id=1, replica_groups=mesh['yhi'=2,'core'=2,'x'=4,'z'=4,'ylo'=2] {'yhi','ylo'}, dimensions={0} | all-to-all | bytes 32768 | tf_op jit(solution)/shard_map/all_to_all | solution.py:23
  68.3 1.2 collective-permute-done.4
  69.5 4.0 %pad_maximum_fusion = bf16[8,128,2048]{2,1,0:T(8,128)(2,1)} fusion(bf16[4,128,2048]{2,1,0:T(8,128)(2,1)} %collective-permute-done, bf16[4,128,2048]{2,1,0:T(8,128)(2,1)S(1)} %all_to_all.15), kind=kLoop, calls=%fused_computation.2 | loop fusion | flops 2097152 | bytes 8388608 | tf_op jit(solution)/shard_map/concatenate | solution.py:44
  73.5 6.7 %all-gather.7.cloned.1.call-done = bf16[32,44,2048]{2,1,0:T(8,128)(2,1)} async-done(((bf16[2,44,2048]{2,1,0:T(8,128)(2,1)}), bf16[32,44,2048]{2,1,0:T(8,128)(2,1)}) %all-gather.7.cloned.1.call-update) | async-done | bytes 5767184 | tf_op jit(solution)/shard_map/all_gather | solution.py:17
  80.2 8.0 %reshape.25 = bf16[1408,2048]{1,0:T(8,128)(2,1)} reshape(bf16[32,44,2048]{2,1,0:T(8,128)(2,1)} %all-gather.7.cloned.1.call-done) | data formatting | bytes 11534336 | tf_op jit(solution)/shard_map/reshape | solution.py:18
  88.2 55.2 %all-gather.9.cloned.1.call-done = bf16[32,44,2048]{2,1,0:T(8,128)(2,1)} async-done(((bf16[2,44,2048]{2,1,0:T(8,128)(2,1)}), bf16[32,44,2048]{2,1,0:T(8,128)(2,1)}) %all-gather.9.cloned.1.call-update) | async-done | bytes 5767184 | tf_op jit(solution)/shard_map/all_gather | solution.py:17
  143.4 8.0 %reshape.26 = bf16[1408,2048]{1,0:T(8,128)(2,1)} reshape(bf16[32,44,2048]{2,1,0:T(8,128)(2,1)} %all-gather.9.cloned.1.call-done) | data formatting | bytes 11534336 | tf_op jit(solution)/shard_map/reshape | solution.py:18
  151.3 11.8 %fusion.3 = f32[1024,1408]{1,0:T(8,128)} fusion(bf16[1024,2048]{1,0:T(8,128)(2,1)} %bitcast.32, bf16[1408,2048]{1,0:T(8,128)(2,1)} %reshape.25), kind=kOutput, calls=%fused_computation.23 | convolution fusion | flops 5905580032 | bytes 15728640 | tf_op jit(solution)/shard_map/dot_general | solution.py:48
  163.1 43.4 %all-gather.11.cloned.1.call-done = bf16[32,44,2048]{2,1,0:T(8,128)(2,1)} async-done(((bf16[2,44,2048]{2,1,0:T(8,128)(2,1)}), bf16[32,44,2048]{2,1,0:T(8,128)(2,1)}) %all-gather.11.cloned.1.call-update) | async-done | bytes 5767184 | tf_op jit(solution)/shard_map/all_gather | solution.py:17
  206.6 8.0 %reshape.27 = bf16[1408,2048]{1,0:T(8,128)(2,1)} reshape(bf16[32,44,2048]{2,1,0:T(8,128)(2,1)} %all-gather.11.cloned.1.call-done) | data formatting | bytes 11534336 | tf_op jit(solution)/shard_map/reshape | solution.py:18
  214.6 21.4 %convert_multiply_fusion = f32[1024,2048]{1,0:T(8,128)} fusion(f32[1024]{0:T(1024)S(1)} %bitcast.41, bf16[1408,2048]{1,0:T(8,128)(2,1)} %reshape.27, f32[1024,1408]{1,0:T(8,128)} %fusion.3, bf16[1024,2048]{1,0:T(8,128)(2,1)} %bitcast.33, bf16[1408,2048]{1,0:T(8,128)(2,1)} %reshape.26), kind=kOutput, calls=%fused_computation | convolution fusion | flops 11826102272 | bytes 29888512 | tf_op jit(solution)/shard_map/dot_general | solution.py:51
  236.0 4.0 %fusion.2 = (f32[512,2048]{1,0:T(8,128)S(1)}, f32[512,2048]{1,0:T(8,128)S(1)}) fusion(f32[1024,2048]{1,0:T(8,128)} %convert_multiply_fusion), kind=kLoop, calls=%fused_computation.22 | loop fusion | bytes 16777216 | tf_op jit(solution)/shard_map/slice | solution.py:54
  240.2 7.1 %collective-permute-done.5 = f32[4,128,2048]{2,1,0:T(8,128)S(1)} collective-permute-done((f32[4,128,2048]{2,1,0:T(8,128)S(1)}, f32[4,128,2048]{2,1,0:T(8,128)S(1)}, u32[]{:S(2)}, u32[]{:S(2)}) %collective-permute-start.5) | collective-permute-done | bytes 4194336 | tf_op jit(solution)/shard_map/ppermute | solution.py:54
  248.3 30.7 %all_to_all.17 = bf16[4,128,2048]{2,1,0:T(8,128)(2,1)S(1)} all-to-all(bf16[4,128,2048]{2,1,0:T(8,128)(2,1)S(1)} %add_convert_fusion), channel_id=1, replica_groups=mesh['yhi'=2,'core'=2,'x'=4,'z'=4,'ylo'=2] {'yhi','ylo'}, dimensions={0} | all-to-all | bytes 4194304 | tf_op jit(solution)/shard_map/all_to_all | solution.py:56
  279.0 1.3 reduce_sum.22
  (31 shorter events, 4.6 us)
Async XLA Ops:
  6.5 25.9 %copy-start = (bf16[128,2048]{1,0:T(8,128)(2,1)S(1)}, bf16[128,2048]{1,0:T(8,128)(2,1)}, u32[]{:S(2)}) copy-start(bf16[128,2048]{1,0:T(8,128)(2,1)} %param.6) | copy-start | bytes 1572868
  6.5 73.6 %all-gather.7.cloned.1.call-start = ((), (), s32[]{:S(2)}) async-start(), calls=%async_computation.3 | async-start | bytes 6684672 | tf_op jit(solution)/shard_map/all_gather | solution.py:17
  8.6 6.6 %collective-permute-start.1 = (bf16[44,2048]{1,0:T(8,128)(2,1)S(1)}, bf16[44,2048]{1,0:T(8,128)(2,1)S(1)}, u32[]{:S(2)}, u32[]{:S(2)}) collective-permute-start(bf16[44,2048]{1,0:T(8,128)(2,1)S(1)} %bitcast.35), channel_id=1, source_target_pairs={{0,1},{1,0},{2,3},{3,2},{4,5},{5,4},{6,7},{7,6},{8,9},{9,8},{10,11... | collective-permute-start | bytes 540680 | tf_op jit(solution)/shard_map/ppermute | solution.py:15
  16.0 127.3 %all-gather.9.cloned.1.call-start = ((), (), s32[]{:S(2)}) async-start(), calls=%async_computation.4 | async-start | bytes 6684672 | tf_op jit(solution)/shard_map/all_gather | solution.py:17
  18.9 41.6 %copy-start.1 = (f32[128,6]{0,1:T(8,128)S(1)}, f32[128,6]{0,1:T(8,128)}, u32[]{:S(2)}) copy-start(f32[128,6]{0,1:T(8,128)} %param.8) | copy-start | bytes 9220
  18.9 41.6 %copy-start.2 = (s32[128,6]{0,1:T(8,128)S(1)}, s32[128,6]{0,1:T(8,128)}, u32[]{:S(2)}) copy-start(s32[128,6]{0,1:T(8,128)} %param.7) | copy-start | bytes 9220
  19.1 5.8 %collective-permute-start.2 = (bf16[44,2048]{1,0:T(8,128)(2,1)S(1)}, bf16[44,2048]{1,0:T(8,128)(2,1)S(1)}, u32[]{:S(2)}, u32[]{:S(2)}) collective-permute-start(bf16[44,2048]{1,0:T(8,128)(2,1)S(1)} %bitcast.37), channel_id=1, source_target_pairs={{0,1},{1,0},{2,3},{3,2},{4,5},{5,4},{6,7},{7,6},{8,9},{9,8},{10,11... | collective-permute-start | bytes 540680 | tf_op jit(solution)/shard_map/ppermute | solution.py:15
  25.7 180.8 %all-gather.11.cloned.1.call-start = ((), (), s32[]{:S(2)}) async-start(), calls=%async_computation.5 | async-start | bytes 6684672 | tf_op jit(solution)/shard_map/all_gather | solution.py:17
  25.9 5.7 %collective-permute-start.3 = (bf16[44,2048]{1,0:T(8,128)(2,1)S(1)}, bf16[44,2048]{1,0:T(8,128)(2,1)S(1)}, u32[]{:S(2)}, u32[]{:S(2)}) collective-permute-start(bf16[44,2048]{1,0:T(8,128)(2,1)S(1)} %bitcast.36), channel_id=1, source_target_pairs={{0,1},{1,0},{2,3},{3,2},{4,5},{5,4},{6,7},{7,6},{8,9},{9,8},{10,11... | collective-permute-start | bytes 540680 | tf_op jit(solution)/shard_map/ppermute | solution.py:15
  60.5 9.0 %collective-permute-start = (bf16[4,128,2048]{2,1,0:T(8,128)(2,1)S(1)}, bf16[4,128,2048]{2,1,0:T(8,128)(2,1)}, u32[]{:S(2)}, u32[]{:S(2)}) collective-permute-start(bf16[4,128,2048]{2,1,0:T(8,128)(2,1)S(1)} %all_to_all.15), channel_id=1, source_target_pairs={{0,32},{32,0},{1,33},{33,1},{2,34},{34,2},{3,35},{35,3},{4,36},{36... | collective-permute-start | bytes 6291464 | tf_op jit(solution)/shard_map/ppermute | solution.py:24
  68.3 1.2 collective-permute-start.4
  240.1 7.2 %collective-permute-start.5 = (f32[4,128,2048]{2,1,0:T(8,128)S(1)}, f32[4,128,2048]{2,1,0:T(8,128)S(1)}, u32[]{:S(2)}, u32[]{:S(2)}) collective-permute-start(f32[4,128,2048]{2,1,0:T(8,128)S(1)} %bitcast.34), channel_id=1, source_target_pairs={{0,32},{32,0},{1,33},{33,1},{2,34},{34,2},{3,35},{35,3},{4,36},{36... | collective-permute-start | bytes 12582920 | tf_op jit(solution)/shard_map/ppermute | solution.py:54
Sparse Core Ops, SparseCore 0:
  16.2 63.9 all-gather.6
  82.3 60.9 all-gather.8
  145.5 60.9 all-gather.10
